TPU v7x, 32 devices: a whole 2x2x4 slice. The times are simulated.
32 devices in a mesh: task: 2 (over y), row: 4 (over z), col: 4 (over x, core).
Axes of the slice: x: 2, y: 2, z: 4, core: 2. Of those that a mesh axis runs over, the one named last changes fastest.
Arguments:
- features: bfloat16 [164, 4096], P(None, ('task', 'row', 'col')), parts along dimension 1, may hold values from -6 to 6
- rung_index: int32 [4096], P(('task', 'row', 'col')), parts along dimension 0, may hold values from 0 to 3
- w_first: bfloat16 [164, 512], replicated, may hold values from -0.5 to 0.5
- b_first: float32 [512], replicated, may hold values from -4 to 4
- w_second: bfloat16 [512, 512], replicated, may hold values from -0.25 to 0.25
- b_second: float32 [512], replicated, may hold values from -4 to 4
- w_third: bfloat16 [512, 64], replicated, may hold values from -0.25 to 0.25
- targets: float32 [16, 4096], P(None, ('task', 'row', 'col')), parts along dimension 1, may hold values from -80 to 80
- fidelity_factor: float32 [8, 4], P('task'), parts along dimension 0, may hold values from -4 to 4
- inverse_scale: float32 [2], P('task'), parts along dimension 0, may hold values from 0.02 to 0.1
- noise_var: float32 [2], P('task'), parts along dimension 0, may hold values from 0.3 to 1
Outputs:
- solution: float32 [16, 4096], P(None, ('task', 'row', 'col')), parts along dimension 1
- residual: float32 [16, 4096], P(None, ('task', 'row', 'col')), parts along dimension 1
There are 2 independent parts, one for each index of `task`. A program takes and returns all parts, laid end to end along the dimension named above; an argument that names none is the same for every part. Nothing has to cross between parts.
All inputs are finite; a program needn't handle non-finite values.
Results may differ from a plain program's by a relative error of at most 0.012.
The roundings to bfloat16 on the way count: a program that leaves them out, or rounds other values in their place, can miss the bound.
Values may be sent and summed in bfloat16 or wider, within the bound.
No kernel may reach another device: no remote copies, remote signals or barrier semaphores. Data moves between devices by JAX's collectives and lax.ppermute only.
A program may use at most 64 MiB of HBM per device.

v0:
```python
import jax
import jax.numpy as jnp
from jax import lax
from jax.sharding import PartitionSpec as P

ITERS = 2


def fidelity_matrix(fidelity_factor):
    lower = jnp.tril(fidelity_factor)
    return jnp.dot(lower, lower.T, precision=lax.Precision.HIGHEST) + 0.5 * jnp.eye(
        fidelity_factor.shape[0], dtype=jnp.float32
    )


def left_product(weights, values):
    return lax.dot_general(
        weights, values, (((0,), (0,)), ((), ())), preferred_element_type=jnp.float32
    )


def outer_gram(left_side, right_side):
    return lax.dot_general(
        left_side, right_side, (((1,), (1,)), ((), ())), precision=lax.Precision.HIGHEST
    )


def solve_spd(matrix, right_side):
    return jax.scipy.linalg.cho_solve((jnp.linalg.cholesky(matrix), True), right_side)


def block_size(total_count, largest):
    chosen = min(total_count, largest)
    while total_count % chosen != 0:
        chosen = chosen - 1
    return chosen


def rung_fidelity(fidelity, rung_value):
    levels = jnp.arange(fidelity.shape[0], dtype=jnp.float32)
    onehot = (rung_value.astype(jnp.float32)[None, :] == levels[:, None]).astype(jnp.float32)
    return jnp.dot(fidelity, onehot, precision=lax.Precision.HIGHEST)


def kernel_image(embedding, squares, rung_value, col_fidelity, inverse_scale, direction):
    count = embedding.shape[1]
    row_block = block_size(count, 2048)
    col_block = block_size(count, 2048)
    levels = jnp.arange(col_fidelity.shape[0], dtype=jnp.float32)

    def one_row_block(block_number):
        first_row = block_number * row_block
        rows_embedding = lax.dynamic_slice_in_dim(embedding, first_row, row_block, 1)
        rows_squares = lax.dynamic_slice_in_dim(squares, first_row, row_block, 0)
        rows_rung = lax.dynamic_slice_in_dim(rung_value, first_row, row_block, 0)
        rows_match = rows_rung.astype(jnp.float32)[:, None] == levels[None, :]

        def one_col_block(running, column_number):
            first_col = column_number * col_block
            cols_embedding = lax.dynamic_slice_in_dim(embedding, first_col, col_block, 1)
            cols_squares = lax.dynamic_slice_in_dim(squares, first_col, col_block, 0)
            cols_fidelity = lax.dynamic_slice_in_dim(col_fidelity, first_col, col_block, 1)
            cols_direction = lax.dynamic_slice_in_dim(direction, first_col, col_block, 1)
            inner = left_product(rows_embedding, cols_embedding)
            distance = rows_squares[:, None] + cols_squares[None, :] - 2.0 * inner
            tile_fidelity = cols_fidelity[0][None, :]
            for level in range(1, col_fidelity.shape[0]):
                tile_fidelity = jnp.where(
                    rows_match[:, level : level + 1], cols_fidelity[level][None, :], tile_fidelity
                )
            kernel = jnp.exp(-inverse_scale[0] * distance) * tile_fidelity
            contribution = lax.dot_general(
                cols_direction, kernel, (((1,), (1,)), ((), ())), precision=lax.Precision.HIGHEST
            )
            return (running + contribution, None)

        start_value = jnp.zeros((direction.shape[0], row_block), jnp.float32)
        result, unused = lax.scan(
            one_col_block, start_value, jnp.arange(count // col_block, dtype=jnp.int32)
        )
        return result

    stacked = lax.map(one_row_block, jnp.arange(count // row_block, dtype=jnp.int32))
    return jnp.transpose(stacked, (1, 0, 2)).reshape(direction.shape[0], count)


def on_device(
    features,
    rung_index,
    w_first,
    b_first,
    w_second,
    b_second,
    w_third,
    targets,
    fidelity_factor,
    inverse_scale,
    noise_var,
):
    fidelity = fidelity_matrix(fidelity_factor)
    hidden_one = jax.nn.silu(left_product(w_first, features) + b_first[:, None]).astype(
        jnp.bfloat16
    )
    hidden_two = jax.nn.silu(left_product(w_second, hidden_one) + b_second[:, None]).astype(
        jnp.bfloat16
    )
    embedding = left_product(w_third, hidden_two).astype(jnp.bfloat16)
    rung_value = rung_index.astype(jnp.float32).astype(jnp.bfloat16)
    own_count = targets.shape[1]
    own_first = (lax.axis_index("row") * lax.axis_size("col") + lax.axis_index("col")) * own_count
    all_embedding = lax.all_gather(embedding, ("row", "col"), axis=1, tiled=True)
    all_rung = lax.all_gather(rung_value, ("row", "col"), axis=0, tiled=True)
    all_targets = lax.all_gather(targets, ("row", "col"), axis=1, tiled=True)
    squares = jnp.sum(jnp.square(all_embedding.astype(jnp.float32)), axis=0)
    col_fidelity = rung_fidelity(fidelity, all_rung)
    solution = jnp.zeros_like(all_targets)
    residual = all_targets
    direction = all_targets
    gram = outer_gram(residual, residual)
    for iteration in range(ITERS):
        image = (
            kernel_image(all_embedding, squares, all_rung, col_fidelity, inverse_scale, direction)
            + noise_var[0] * direction
        )
        curvature = outer_gram(direction, image)
        step_matrix = solve_spd(curvature, gram)
        solution = solution + jnp.dot(step_matrix.T, direction, precision=lax.Precision.HIGHEST)
        residual = residual - jnp.dot(step_matrix.T, image, precision=lax.Precision.HIGHEST)
        if iteration + 1 < ITERS:
            new_gram = outer_gram(residual, residual)
            update_matrix = solve_spd(gram, new_gram)
            direction = residual + jnp.dot(
                update_matrix.T, direction, precision=lax.Precision.HIGHEST
            )
            gram = new_gram
    own_solution = lax.dynamic_slice_in_dim(solution, own_first, own_count, 1)
    own_residual = lax.dynamic_slice_in_dim(residual, own_first, own_count, 1)
    return (own_solution, own_residual)


def solution(mesh):
    placed = (
        P(None, ("task", "row", "col")),
        P(("task", "row", "col")),
        P(),
        P(),
        P(),
        P(),
        P(),
        P(None, ("task", "row", "col")),
        P("task", None),
        P("task"),
        P("task"),
    )
    return jax.shard_map(
        on_device,
        mesh=mesh,
        in_specs=placed,
        out_specs=(P(None, ("task", "row", "col")), P(None, ("task", "row", "col"))),
        check_vma=False,
    )
```

profile of v0, /device:TPU:0, one launch (start us, length us, event | category | flops | bytes accessed | tf_op | source)
XLA Modules:
  0.0 122.0 jit_solution(9418712131245514869)
XLA Ops:
  0.6 0.0 copy-start
  0.6 0.7 convert_bitcast_fusion
  1.4 23.1 %all-gather = bf16[16,1,128]{2,1,0:T(2,128)(2,1)S(1)} all-gather(bf16[1,1,128]{2,1,0:T(2,128)(2,1)S(1)} %convert_bitcast_fusion), channel_id=1, replica_groups=mesh['task'=2,'row'=4,'col'=4] {'row','col'}, dimensions={0}, use_global_device_ids=true | all-gather | bytes 4352 | tf_op jit(solution)/shard_map/all_gather | solution.py:112
  24.5 0.9 convolution_add_fusion.4
  25.3 0.2 fusion.5
  25.6 0.1 slice_reduce_fusion.2
  25.7 1.3 %multiply_convert_fusion.1 = bf16[512,128]{1,0:T(8,128)(2,1)S(1)} fusion(bf16[164,512]{1,0:T(8,128)(2,1)} %param.16, bf16[164,128]{1,0:T(8,128)(2,1)} %param.14, f32[512]{0:T(512)} %param.17), kind=kOutput, calls=%fused_computation.14 | convolution fusion | flops 21889024 | bytes 343040 | tf_op jit(solution)/shard_map/dot_general | solution.py:17
  26.9 1.4 %fusion.2 = bf16[64,128]{1,0:T(8,128)(2,1)S(1)} fusion(bf16[512,64]{0,1:T(8,128)(2,1)} %param.20, bf16[512,128]{1,0:T(8,128)(2,1)S(1)} %multiply_convert_fusion.1, bf16[512,512]{1,0:T(8,128)(2,1)S(1)} %copy-done, f32[512]{0:T(512)} %param.19), kind=kOutput, calls=%fused_computation.10 | convolution fusion | flops 75898880 | bytes 739328 | tf_op jit(solution)/shard_map/dot_general | solution.py:17
  28.3 18.2 %all_gather.9 = bf16[64,2048]{1,0:T(8,128)(2,1)S(1)} all-gather(bf16[64,128]{1,0:T(8,128)(2,1)S(1)} %fusion.2), channel_id=1, replica_groups=mesh['task'=2,'row'=4,'col'=4] {'row','col'}, dimensions={1}, use_global_device_ids=true | all-gather | bytes 278528 | tf_op jit(solution)/shard_map/all_gather | solution.py:111
  46.4 0.1 multiply_reduce_fusion
  47.2 0.0 copy-start.2
  47.2 6.6 %select_multiply_fusion = f32[2048,2048]{1,0:T(8,128)S(1)} fusion(bf16[64,2048]{1,0:T(8,128)(2,1)S(1)} %all_gather.9, f32[2048]{0:T(1024)S(1)} %bitcast.95, f32[2048]{0:T(1024)S(1)} %bitcast.96, f32[2048]{0:T(1024)S(1)} %bitcast.97, f32[2048]{0:T(1024)S(1)} %bitcast.94, f32[2048]{0:T(1024)S(1)} %multiply_reduce_fusion, f32[]{:T(128)} %bitcast, ...), kind=kOutput, calls=%fused_computation | convolution fusion | flops 570425344 | bytes 17086468 | tf_op jit(solution)/shard_map/while/body/eval_jaxpr/while/body/eval_jaxpr/dot_general | solution.py:17
  53.8 0.0 copy-done.2
  53.8 19.3 %all_gather.11 = f32[16,2048]{1,0:T(8,128)S(1)} all-gather(f32[16,128]{1,0:T(8,128)S(1)} %copy-done.2), channel_id=1, replica_groups=mesh['task'=2,'row'=4,'col'=4] {'row','col'}, dimensions={1}, use_global_device_ids=true | all-gather | bytes 139264 | tf_op jit(solution)/shard_map/all_gather | solution.py:113
  73.7 0.0 copy-done.1
  73.8 14.1 %fusion = f32[16,2048]{1,0:T(8,128)S(1)} fusion(f32[2048,2048]{1,0:T(8,128)S(1)} %select_multiply_fusion, f32[16,2048]{1,0:T(8,128)S(1)} %all_gather.11, f32[]{:T(128)} %bitcast.89), kind=kOutput, calls=%fused_computation.5 | convolution fusion | flops 805371904 | bytes 17039364 | tf_op jit(solution)/shard_map/while/body/eval_jaxpr/while/body/eval_jaxpr/dot_general | solution.py:72
  87.9 0.2 fusion.29
  88.1 0.1 copy.22
  88.2 1.5 %cholesky.59 = f32[16,16]{1,0:T(8,128)S(1)} custom-call(f32[16,16]{1,0:T(8,128)S(1)} %add_multiply_fusion), custom_call_target="Cholesky" | custom-call | tf_op jit(solution)/shard_map/jit(cholesky)/cholesky | solution.py:29
  89.8 0.6 compare_reduce_fusion.2
  90.4 0.6 fusion.7
  91.1 1.2 %custom-call.9 = f32[1,16,16]{1,2,0:T(8,128)S(1)} custom-call(f32[1,16,16]{2,1,0:T(8,128)S(1)} %fusion.7), custom_call_target="InvertDiagBlocksLowerTriangular" | custom-call | tf_op jit(solution)/shard_map/jit(_cho_solve)/triangular_solve | solution.py:29
  92.3 0.2 fusion.30
  92.5 0.3 fusion.22
  92.8 0.1 fusion.20
  93.0 0.3 convolution_subtract_fusion
  93.3 0.4 fusion.32
  93.7 0.1 copy.23
  93.8 1.5 %cholesky.70 = f32[16,16]{1,0:T(8,128)S(1)} custom-call(f32[16,16]{1,0:T(8,128)S(1)} %fusion.19), custom_call_target="Cholesky" | custom-call | tf_op jit(solution)/shard_map/jit(cholesky)/cholesky | solution.py:29
  95.4 0.6 compare_reduce_fusion.1
  96.0 0.6 fusion.8
  96.7 1.2 %custom-call.10 = f32[1,16,16]{1,2,0:T(8,128)S(1)} custom-call(f32[1,16,16]{2,1,0:T(8,128)S(1)} %fusion.8), custom_call_target="InvertDiagBlocksLowerTriangular" | custom-call | tf_op jit(solution)/shard_map/jit(_cho_solve)/triangular_solve | solution.py:29
  97.9 0.2 fusion.17
  98.1 0.1 fusion.15
  98.2 0.3 convolution_add_fusion
  98.6 17.1 %convolution_add_fusion.1 = f32[16,2048]{1,0:T(8,128)S(1)} fusion(f32[16,2048]{1,0:T(8,128)S(1)} %convolution_add_fusion, f32[2048,2048]{1,0:T(8,128)} %copy-done.1, f32[]{:T(128)} %bitcast.90), kind=kOutput, calls=%fused_computation.3 | convolution fusion | flops 805371904 | bytes 17039364 | tf_op jit(solution)/shard_map/while/body/eval_jaxpr/while/body/eval_jaxpr/dot_general | solution.py:72
  115.7 0.2 fusion.33
  115.9 0.1 copy.24
  116.0 1.5 %cholesky.81 = f32[16,16]{1,0:T(8,128)S(1)} custom-call(f32[16,16]{1,0:T(8,128)S(1)} %fusion.14), custom_call_target="Cholesky" | custom-call | tf_op jit(solution)/shard_map/jit(cholesky)/cholesky | solution.py:29
  117.5 0.6 compare_reduce_fusion
  118.2 0.6 fusion.9
  118.9 1.2 %custom-call.11 = f32[1,16,16]{1,2,0:T(8,128)S(1)} custom-call(f32[1,16,16]{2,1,0:T(8,128)S(1)} %fusion.9), custom_call_target="InvertDiagBlocksLowerTriangular" | custom-call | tf_op jit(solution)/shard_map/jit(_cho_solve)/triangular_solve | solution.py:29
  120.1 0.2 fusion.12
  120.3 0.1 fusion.10
  120.4 0.3 fusion.34
  120.8 0.3 fusion.35
  121.1 0.3 fusion.31
  121.4 0.6 dynamic-slice_subtract_fusion
  (11 shorter events, 0.2 us)
Async XLA Ops:
  0.6 26.3 %copy-start = (bf16[512,512]{1,0:T(8,128)(2,1)S(1)}, bf16[512,512]{1,0:T(8,128)(2,1)}, u32[]{:S(2)}) copy-start(bf16[512,512]{1,0:T(8,128)(2,1)} %param.18) | copy-start | bytes 1572868
  47.2 6.6 %copy-start.2 = (f32[16,128]{1,0:T(8,128)S(1)}, f32[16,128]{1,0:T(8,128)}, u32[]{:S(2)}) copy-start(f32[16,128]{1,0:T(8,128)} %param.21) | copy-start | bytes 24580
  53.8 20.0 %copy-start.1 = (f32[2048,2048]{1,0:T(8,128)}, f32[2048,2048]{1,0:T(8,128)S(1)}, u32[]{:S(2)}) copy-start(f32[2048,2048]{1,0:T(8,128)S(1)} %select_multiply_fusion) | copy-start | bytes 50331652
where the time goes:
time: 122 us
  blocking collectives  60.5 us (50%)
  matrix products  45.3 us (37%)
  other arithmetic  13.7 us (11%)
  between operations  2.14 us (2%)
    dot_general x2, matrix products, one_col_block(): lax.dot_general(cols_direction, kernel, (((1,), (1,)), ((), ())), precisi...  31.2 us
    all_gather x1, blocking collectives, on_device(): all_rung = lax.all_gather(rung_value, ('row', 'col'), axis=0, tiled=True)  23.1 us
    all_gather x1, blocking collectives, on_device(): all_targets = lax.all_gather(targets, ('row', 'col'), axis=1, tiled=True)  19.3 us
    all_gather x1, blocking collectives, on_device(): lax.all_gather(embedding, ('row', 'col'), axis=1, tiled=True)  18.2 us
    dot_general x3, matrix products, left_product(): lax.dot_general(weights, values, (((0,), (0,)), ((), ())), preferred_elem...  9.19 us
    another operation x9, other arithmetic, solve_spd(): jnp.linalg.cholesky(matrix)  6.57 us
    another operation x6, other arithmetic, solve_spd(): jax.scipy.linalg.cho_solve((jnp.linalg.cholesky(matrix), True), right_side)  5.63 us

commit v1 on v0

--- a/solution.py
+++ b/solution.py
@@ -110,7 +110,35 @@
     own_first = (lax.axis_index("row") * lax.axis_size("col") + lax.axis_index("col")) * own_count
     all_embedding = lax.all_gather(embedding, ("row", "col"), axis=1, tiled=True)
     all_rung = lax.all_gather(rung_value, ("row", "col"), axis=0, tiled=True)
-    all_targets = lax.all_gather(targets, ("row", "col"), axis=1, tiled=True)
+    tmp, current_arr, base_arr = (
+        lax.axis_size(("row", "col")),
+        lax.axis_index(("row", "col")),
+        targets.shape[1],
+    )
+    lanes = []
+    for p in range(tmp):
+        lanes.append((p, (p + 1) % tmp))
+    inbox = []
+    for p in range(tmp):
+        inbox.append((p, (p - 1) % tmp))
+    all_targets = jnp.zeros(
+        (*targets.shape[:1], tmp * base_arr, *targets.shape[1 + 1 :]), targets.dtype
+    )
+    all_targets = lax.dynamic_update_slice_in_dim(
+        all_targets, targets, current_arr * base_arr, axis=1
+    )
+    taken_in = block_next = targets
+    v_next = tmp // 2
+    for d in range(1, v_next + 1):
+        taken_in = lax.ppermute(taken_in, ("row", "col"), perm=lanes)
+        all_targets = lax.dynamic_update_slice_in_dim(
+            all_targets, taken_in, (current_arr - d) % tmp * base_arr, axis=1
+        )
+        if d < tmp - v_next:
+            block_next = lax.ppermute(block_next, ("row", "col"), inbox)
+            all_targets = lax.dynamic_update_slice_in_dim(
+                all_targets, block_next, (current_arr + d) % tmp * base_arr, axis=1
+            )
     squares = jnp.sum(jnp.square(all_embedding.astype(jnp.float32)), axis=0)
     col_fidelity = rung_fidelity(fidelity, all_rung)
     solution = jnp.zeros_like(all_targets)

time: 122 us -> 153 us (1.25)
  starting transfers between devices: 0 us -> 28.5 us
  blocking collectives: 60.5 us -> 37 us
  waiting for transfers between devices: 0 us -> 18.4 us
  matrix products: 45.3 us -> 52.2 us
    ppermute x0 -> x15, starting transfers between devices: none -> 28.5 us  [the longest x7 28.5 us: on_device(): block_next = lax.ppermute(block_next, ('row', 'col'), inbox)]
    all_gather x1 -> x0, blocking collectives: 19.3 us -> none  [on_device(): all_targets = lax.all_gather(targets, ('row', 'col'), axis=1, tiled=True)]
    ppermute x0 -> x15, waiting for transfers between devices: none -> 18.4 us  [the longest x8 11.8 us: on_device(): taken_in = lax.ppermute(taken_in, ('row', 'col'), perm=lanes)]
    all_gather x1, blocking collectives: 23.1 us -> 18.2 us  [on_device(): all_rung = lax.all_gather(rung_value, ('row', 'col'), axis=0, tiled=True)]
    dot_general x3, matrix products: 9.19 us -> 13.1 us  [left_product(): lax.dot_general(weights, values, (((0,), (0,)), ((), ())), preferred_elem...]
    dot_general x2, matrix products: 31.2 us -> 34.4 us  [one_col_block(): lax.dot_general(cols_direction, kernel, (((1,), (1,)), ((), ())), precisi...]
  transfers between devices with their start and end apart: 0 -> 15, of which waited for: 0 -> 12; matrix products, arithmetic and copies ran while one was open for 0% -> 10% of each run, Pallas kernels for 0% -> 0%
where the time goes in v1:
time: 153 us
  matrix products  52.2 us (34%)
  blocking collectives  37 us (24%)
  starting transfers between devices  28.5 us (19%)
  waiting for transfers between devices  18.4 us (12%)
  other arithmetic  13.5 us (9%)
  between operations  2.2 us (1%)
    dot_general x2, matrix products, one_col_block(): lax.dot_general(cols_direction, kernel, (((1,), (1,)), ((), ())), precisi...  34.4 us
    ppermute x7, starting transfers between devices, on_device(): block_next = lax.ppermute(block_next, ('row', 'col'), inbox)  28.5 us
    all_gather x1, blocking collectives, on_device(): lax.all_gather(embedding, ('row', 'col'), axis=1, tiled=True)  18.9 us
    all_gather x1, blocking collectives, on_device(): all_rung = lax.all_gather(rung_value, ('row', 'col'), axis=0, tiled=True)  18.2 us
    dot_general x3, matrix products, left_product(): lax.dot_general(weights, values, (((0,), (0,)), ((), ())), preferred_elem...  13.1 us
    ppermute x8, waiting for transfers between devices, on_device(): taken_in = lax.ppermute(taken_in, ('row', 'col'), perm=lanes)  11.8 us
    ppermute x7, waiting for transfers between devices, on_device(): block_next = lax.ppermute(block_next, ('row', 'col'), inbox)  6.52 us
    another operation x9, other arithmetic, solve_spd(): jnp.linalg.cholesky(matrix)  6.51 us
  transfers between devices with their start and end apart: 15, of which 12 were waited for; matrix products, arithmetic and copies ran while one was open for 10% of the time, Pallas kernels for 0%

profile of v1, /device:TPU:0, one launch (start us, length us, event | category | flops | bytes accessed | tf_op | source)
XLA Modules:
  0.0 153.0 jit_solution(3476453525820292596)
XLA Ops:
  0.6 5.5 %collective-permute-start.1 = (f32[16,128]{1,0:T(8,128)}, f32[16,128]{1,0:T(8,128)S(1)}, u32[]{:S(2)}, u32[]{:S(2)}) collective-permute-start(f32[16,128]{1,0:T(8,128)} %param.21), channel_id=1, source_target_pairs={{0,15},{1,0},{2,1},{3,2},{4,3},{5,4},{6,5},{7,6},{8,7},{9,8},{10,9... | collective-permute-start | bytes 24584 | tf_op jit(solution)/shard_map/ppermute | solution.py:138
  6.8 0.7 convert_bitcast_fusion
  7.5 0.9 convolution_add_fusion.4
  8.3 18.2 %all-gather = bf16[16,1,128]{2,1,0:T(2,128)(2,1)S(1)} all-gather(bf16[1,1,128]{2,1,0:T(2,128)(2,1)S(1)} %convert_bitcast_fusion), channel_id=1, replica_groups=mesh['task'=2,'row'=4,'col'=4] {'row','col'}, dimensions={0}, use_global_device_ids=true | all-gather | bytes 4352 | tf_op jit(solution)/shard_map/all_gather | solution.py:112
  26.8 1.3 multiply_convert_fusion.1
  28.1 1.3 fusion.1
  29.4 18.9 %all_gather.6 = bf16[64,2048]{1,0:T(8,128)(2,1)S(1)} all-gather(bf16[64,128]{1,0:T(8,128)(2,1)S(1)} %fusion.1), channel_id=1, replica_groups=mesh['task'=2,'row'=4,'col'=4] {'row','col'}, dimensions={1}, use_global_device_ids=true | all-gather | bytes 278528 | tf_op jit(solution)/shard_map/all_gather | solution.py:111
  48.4 0.7 constant_dynamic-update-slice_fusion.15
  49.1 10.5 %select_multiply_fusion = f32[2048,2048]{1,0:T(8,128)} fusion(bf16[64,2048]{1,0:T(8,128)(2,1)S(1)} %all_gather.6, f32[2048]{0:T(1024)S(1)} %bitcast.90, f32[2048]{0:T(1024)S(1)} %bitcast.91, f32[2048]{0:T(1024)S(1)} %bitcast.92, f32[2048]{0:T(1024)S(1)} %bitcast.89, f32[2048]{0:T(1024)S(1)} %multiply_reduce_fusion, f32[]{:T(128)} %bitcast, ...), kind=kOutput, calls=%fused_computation | convolution fusion | flops 570425344 | bytes 17086468 | tf_op jit(solution)/shard_map/while/body/eval_jaxpr/while/body/eval_jaxpr/dot_general | solution.py:17
  60.4 0.9 collective-permute-start.3
  61.3 1.3 collective-permute-done.3
  62.7 4.4 %collective-permute-start.5 = (f32[16,128]{1,0:T(8,128)S(1)}, f32[16,128]{1,0:T(8,128)S(1)}, u32[]{:S(2)}, u32[]{:S(2)}) collective-permute-start(f32[16,128]{1,0:T(8,128)S(1)} %collective-permute-done.3), channel_id=1, source_target_pairs={{0,15},{1,0},{2,1},{3,2},{4,3},{5,4},{6,5},{7,6},{8,7},{9,8},{10,9... | collective-permute-start | bytes 24584 | tf_op jit(solution)/shard_map/ppermute | solution.py:138
  67.2 1.3 collective-permute-done.5
  68.5 4.4 %collective-permute-start.7 = (f32[16,128]{1,0:T(8,128)S(1)}, f32[16,128]{1,0:T(8,128)S(1)}, u32[]{:S(2)}, u32[]{:S(2)}) collective-permute-start(f32[16,128]{1,0:T(8,128)S(1)} %collective-permute-done.5), channel_id=1, source_target_pairs={{0,15},{1,0},{2,1},{3,2},{4,3},{5,4},{6,5},{7,6},{8,7},{9,8},{10,9... | collective-permute-start | bytes 24584 | tf_op jit(solution)/shard_map/ppermute | solution.py:138
  72.9 1.3 collective-permute-done.7
  74.2 4.4 %collective-permute-start.9 = (f32[16,128]{1,0:T(8,128)S(1)}, f32[16,128]{1,0:T(8,128)S(1)}, u32[]{:S(2)}, u32[]{:S(2)}) collective-permute-start(f32[16,128]{1,0:T(8,128)S(1)} %collective-permute-done.7), channel_id=1, source_target_pairs={{0,15},{1,0},{2,1},{3,2},{4,3},{5,4},{6,5},{7,6},{8,7},{9,8},{10,9... | collective-permute-start | bytes 24584 | tf_op jit(solution)/shard_map/ppermute | solution.py:138
  78.7 1.3 collective-permute-done.9
  80.0 4.4 %collective-permute-start.11 = (f32[16,128]{1,0:T(8,128)S(1)}, f32[16,128]{1,0:T(8,128)S(1)}, u32[]{:S(2)}, u32[]{:S(2)}) collective-permute-start(f32[16,128]{1,0:T(8,128)S(1)} %collective-permute-done.9), channel_id=1, source_target_pairs={{0,15},{1,0},{2,1},{3,2},{4,3},{5,4},{6,5},{7,6},{8,7},{9,8},{10,9... | collective-permute-start | bytes 24584 | tf_op jit(solution)/shard_map/ppermute | solution.py:138
  84.5 1.3 collective-permute-done.11
  85.8 4.4 %collective-permute-start.13 = (f32[16,128]{1,0:T(8,128)S(1)}, f32[16,128]{1,0:T(8,128)S(1)}, u32[]{:S(2)}, u32[]{:S(2)}) collective-permute-start(f32[16,128]{1,0:T(8,128)S(1)} %collective-permute-done.11), channel_id=1, source_target_pairs={{0,15},{1,0},{2,1},{3,2},{4,3},{5,4},{6,5},{7,6},{8,7},{9,8},{10,9... | collective-permute-start | bytes 24584 | tf_op jit(solution)/shard_map/ppermute | solution.py:138
  90.3 5.8 %collective-permute-done.12 = f32[16,128]{1,0:T(8,128)S(1)} collective-permute-done((f32[16,128]{1,0:T(8,128)S(1)}, f32[16,128]{1,0:T(8,128)S(1)}, u32[]{:S(2)}, u32[]{:S(2)}) %collective-permute-start.12) | collective-permute-done | bytes 8224 | tf_op jit(solution)/shard_map/ppermute | solution.py:133
  96.1 5.7 %collective-permute-done.14 = f32[16,128]{1,0:T(8,128)S(1)} collective-permute-done((f32[16,128]{1,0:T(8,128)S(1)}, f32[16,128]{1,0:T(8,128)S(1)}, u32[]{:S(2)}, u32[]{:S(2)}) %collective-permute-start.14) | collective-permute-done | bytes 8224 | tf_op jit(solution)/shard_map/ppermute | solution.py:133
  101.8 0.2 fusion.34
  102.1 17.1 %convolution_add_fusion.1 = f32[16,2048]{1,0:T(8,128)S(1)} fusion(f32[16,2048]{1,0:T(8,128)S(1)} %constant_dynamic-update-slice_fusion, f32[2048,2048]{1,0:T(8,128)} %select_multiply_fusion, f32[]{:T(128)} %bitcast.84), kind=kOutput, calls=%fused_computation.3 | convolution fusion | flops 805371904 | bytes 17039364 | tf_op jit(solution)/shard_map/while/body/eval_jaxpr/while/body/eval_jaxpr/dot_general | solution.py:72
  119.3 0.2 fusion.33
  119.6 1.5 cholesky.59
  121.1 0.6 compare_reduce_fusion.2
  121.8 0.6 fusion.10
  122.4 1.2 custom-call.9
  123.7 0.2 fusion.25
  124.0 0.3 convolution_subtract_fusion
  124.4 0.3 fusion.35
  124.7 1.4 cholesky.70
  126.2 0.6 compare_reduce_fusion.1
  126.8 0.6 fusion.11
  127.5 1.2 custom-call.10
  128.7 0.2 fusion.36
  128.9 0.3 fusion.20
  129.3 0.3 convolution_add_fusion
  129.7 17.3 %fusion.37 = f32[16,2048]{1,0:T(8,128)S(1)} fusion(f32[16,2048]{1,0:T(8,128)S(1)} %convolution_add_fusion, f32[2048,2048]{1,0:T(8,128)} %select_multiply_fusion), kind=kOutput, calls=%fused_computation.89 | convolution fusion | flops 805306368 | bytes 17039360 | tf_op jit(solution)/shard_map/while/body/eval_jaxpr/while/body/eval_jaxpr/dot_general | solution.py:72
  146.9 0.3 fusion.5
  147.3 1.5 cholesky.81
  148.8 0.6 compare_reduce_fusion
  149.5 0.6 fusion.12
  150.2 1.2 custom-call.11
  151.7 0.3 fusion.38
  152.1 0.3 fusion.4
  152.4 0.6 dynamic-slice_subtract_fusion
  (53 shorter events, 1.8 us)
Async XLA Ops:
  0.6 27.5 %copy-start = (bf16[512,512]{1,0:T(8,128)(2,1)S(1)}, bf16[512,512]{1,0:T(8,128)(2,1)}, u32[]{:S(2)}) copy-start(bf16[512,512]{1,0:T(8,128)(2,1)} %param.18) | copy-start | bytes 1572868
  0.6 59.7 %collective-permute-start.1 = (f32[16,128]{1,0:T(8,128)}, f32[16,128]{1,0:T(8,128)S(1)}, u32[]{:S(2)}, u32[]{:S(2)}) collective-permute-start(f32[16,128]{1,0:T(8,128)} %param.21), channel_id=1, source_target_pairs={{0,15},{1,0},{2,1},{3,2},{4,3},{5,4},{6,5},{7,6},{8,7},{9,8},{10,9... | collective-permute-start | bytes 24584 | tf_op jit(solution)/shard_map/ppermute | solution.py:138
  6.1 55.2 %collective-permute-start = (f32[16,128]{1,0:T(8,128)}, f32[16,128]{1,0:T(8,128)S(1)}, u32[]{:S(2)}, u32[]{:S(2)}) collective-permute-start(f32[16,128]{1,0:T(8,128)} %param.21), channel_id=1, source_target_pairs={{0,1},{1,2},{2,3},{3,4},{4,5},{5,6},{6,7},{7,8},{8,9},{9,10},{10,1... | collective-permute-start | bytes 24584 | tf_op jit(solution)/shard_map/ppermute | solution.py:133
  60.4 2.3 %collective-permute-start.3 = (f32[16,128]{1,0:T(8,128)S(1)}, f32[16,128]{1,0:T(8,128)S(1)}, u32[]{:S(2)}, u32[]{:S(2)}) collective-permute-start(f32[16,128]{1,0:T(8,128)S(1)} %collective-permute-done.1), channel_id=1, source_target_pairs={{0,15},{1,0},{2,1},{3,2},{4,3},{5,4},{6,5},{7,6},{8,7},{9,8},{10,9... | collective-permute-start | bytes 24584 | tf_op jit(solution)/shard_map/ppermute | solution.py:138
  61.3 5.9 %collective-permute-start.2 = (f32[16,128]{1,0:T(8,128)S(1)}, f32[16,128]{1,0:T(8,128)S(1)}, u32[]{:S(2)}, u32[]{:S(2)}) collective-permute-start(f32[16,128]{1,0:T(8,128)S(1)} %collective-permute-done), channel_id=1, source_target_pairs={{0,1},{1,2},{2,3},{3,4},{4,5},{5,6},{6,7},{7,8},{8,9},{9,10},{10,1... | collective-permute-start | bytes 24584 | tf_op jit(solution)/shard_map/ppermute | solution.py:133
  62.7 5.8 %collective-permute-start.5 = (f32[16,128]{1,0:T(8,128)S(1)}, f32[16,128]{1,0:T(8,128)S(1)}, u32[]{:S(2)}, u32[]{:S(2)}) collective-permute-start(f32[16,128]{1,0:T(8,128)S(1)} %collective-permute-done.3), channel_id=1, source_target_pairs={{0,15},{1,0},{2,1},{3,2},{4,3},{5,4},{6,5},{7,6},{8,7},{9,8},{10,9... | collective-permute-start | bytes 24584 | tf_op jit(solution)/shard_map/ppermute | solution.py:138
  67.2 5.8 %collective-permute-start.4 = (f32[16,128]{1,0:T(8,128)S(1)}, f32[16,128]{1,0:T(8,128)S(1)}, u32[]{:S(2)}, u32[]{:S(2)}) collective-permute-start(f32[16,128]{1,0:T(8,128)S(1)} %collective-permute-done.2), channel_id=1, source_target_pairs={{0,1},{1,2},{2,3},{3,4},{4,5},{5,6},{6,7},{7,8},{8,9},{9,10},{10,1... | collective-permute-start | bytes 24584 | tf_op jit(solution)/shard_map/ppermute | solution.py:133
  68.5 5.8 %collective-permute-start.7 = (f32[16,128]{1,0:T(8,128)S(1)}, f32[16,128]{1,0:T(8,128)S(1)}, u32[]{:S(2)}, u32[]{:S(2)}) collective-permute-start(f32[16,128]{1,0:T(8,128)S(1)} %collective-permute-done.5), channel_id=1, source_target_pairs={{0,15},{1,0},{2,1},{3,2},{4,3},{5,4},{6,5},{7,6},{8,7},{9,8},{10,9... | collective-permute-start | bytes 24584 | tf_op jit(solution)/shard_map/ppermute | solution.py:138
  72.9 5.8 %collective-permute-start.6 = (f32[16,128]{1,0:T(8,128)S(1)}, f32[16,128]{1,0:T(8,128)S(1)}, u32[]{:S(2)}, u32[]{:S(2)}) collective-permute-start(f32[16,128]{1,0:T(8,128)S(1)} %collective-permute-done.4), channel_id=1, source_target_pairs={{0,1},{1,2},{2,3},{3,4},{4,5},{5,6},{6,7},{7,8},{8,9},{9,10},{10,1... | collective-permute-start | bytes 24584 | tf_op jit(solution)/shard_map/ppermute | solution.py:133
  74.2 5.8 %collective-permute-start.9 = (f32[16,128]{1,0:T(8,128)S(1)}, f32[16,128]{1,0:T(8,128)S(1)}, u32[]{:S(2)}, u32[]{:S(2)}) collective-permute-start(f32[16,128]{1,0:T(8,128)S(1)} %collective-permute-done.7), channel_id=1, source_target_pairs={{0,15},{1,0},{2,1},{3,2},{4,3},{5,4},{6,5},{7,6},{8,7},{9,8},{10,9... | collective-permute-start | bytes 24584 | tf_op jit(solution)/shard_map/ppermute | solution.py:138
  78.7 5.8 %collective-permute-start.8 = (f32[16,128]{1,0:T(8,128)S(1)}, f32[16,128]{1,0:T(8,128)S(1)}, u32[]{:S(2)}, u32[]{:S(2)}) collective-permute-start(f32[16,128]{1,0:T(8,128)S(1)} %collective-permute-done.6), channel_id=1, source_target_pairs={{0,1},{1,2},{2,3},{3,4},{4,5},{5,6},{6,7},{7,8},{8,9},{9,10},{10,1... | collective-permute-start | bytes 24584 | tf_op jit(solution)/shard_map/ppermute | solution.py:133
  80.0 5.8 %collective-permute-start.11 = (f32[16,128]{1,0:T(8,128)S(1)}, f32[16,128]{1,0:T(8,128)S(1)}, u32[]{:S(2)}, u32[]{:S(2)}) collective-permute-start(f32[16,128]{1,0:T(8,128)S(1)} %collective-permute-done.9), channel_id=1, source_target_pairs={{0,15},{1,0},{2,1},{3,2},{4,3},{5,4},{6,5},{7,6},{8,7},{9,8},{10,9... | collective-permute-start | bytes 24584 | tf_op jit(solution)/shard_map/ppermute | solution.py:138
  84.5 5.8 %collective-permute-start.10 = (f32[16,128]{1,0:T(8,128)S(1)}, f32[16,128]{1,0:T(8,128)S(1)}, u32[]{:S(2)}, u32[]{:S(2)}) collective-permute-start(f32[16,128]{1,0:T(8,128)S(1)} %collective-permute-done.8), channel_id=1, source_target_pairs={{0,1},{1,2},{2,3},{3,4},{4,5},{5,6},{6,7},{7,8},{8,9},{9,10},{10,1... | collective-permute-start | bytes 24584 | tf_op jit(solution)/shard_map/ppermute | solution.py:133
  85.8 10.3 %collective-permute-start.13 = (f32[16,128]{1,0:T(8,128)S(1)}, f32[16,128]{1,0:T(8,128)S(1)}, u32[]{:S(2)}, u32[]{:S(2)}) collective-permute-start(f32[16,128]{1,0:T(8,128)S(1)} %collective-permute-done.11), channel_id=1, source_target_pairs={{0,15},{1,0},{2,1},{3,2},{4,3},{5,4},{6,5},{7,6},{8,7},{9,8},{10,9... | collective-permute-start | bytes 24584 | tf_op jit(solution)/shard_map/ppermute | solution.py:138
  90.3 5.8 %collective-permute-start.12 = (f32[16,128]{1,0:T(8,128)S(1)}, f32[16,128]{1,0:T(8,128)S(1)}, u32[]{:S(2)}, u32[]{:S(2)}) collective-permute-start(f32[16,128]{1,0:T(8,128)S(1)} %collective-permute-done.10), channel_id=1, source_target_pairs={{0,1},{1,2},{2,3},{3,4},{4,5},{5,6},{6,7},{7,8},{8,9},{9,10},{10,1... | collective-permute-start | bytes 24584 | tf_op jit(solution)/shard_map/ppermute | solution.py:133
  96.0 5.8 %collective-permute-start.14 = (f32[16,128]{1,0:T(8,128)S(1)}, f32[16,128]{1,0:T(8,128)S(1)}, u32[]{:S(2)}, u32[]{:S(2)}) collective-permute-start(f32[16,128]{1,0:T(8,128)S(1)} %collective-permute-done.12), channel_id=1, source_target_pairs={{0,1},{1,2},{2,3},{3,4},{4,5},{5,6},{6,7},{7,8},{8,9},{9,10},{10,1... | collective-permute-start | bytes 24584 | tf_op jit(solution)/shard_map/ppermute | solution.py:133
